TPU v7x, 512 devices: a whole 4x4x16 slice. The times are simulated.
512 devices in a mesh: seq: 8 (over x, core), tp: 16 (over z), req: 4 (over y).
Axes of the slice: x: 4, y: 4, z: 16, core: 2. Of those that a mesh axis runs over, the one named last changes fastest.
Arguments:
- tokens: bfloat16 [32768, 1792], P(('req', 'seq'), 'tp'), parts along dimension 0, may hold values from -6 to 6
- w_in: bfloat16 [1792, 4096], P(None, 'tp'), may hold values from -0.125 to 0.125
- conv_w: float32 [3, 1792], P(None, 'tp'), may hold values from -3 to 3
- head_gain: float32 [1792], P('tp'), may hold values from 0.1 to 1.9
- w_out: bfloat16 [1792, 1792], P('tp'), may hold values from -0.125 to 0.125
- prompt_lens: int32 [16], P('req'), parts along dimension 0, may hold values from 1 to 4096, 8192 in all
- req_group: int32 [128], P('req'), parts along dimension 0, may hold values from 0 to 3, as said below
- row_request: int32 [128], P('req'), parts along dimension 0, may hold values from 0 to 31, each once
Outputs:
- mixed: bfloat16 [32768, 1792], P(('req', 'seq'), 'tp'), parts along dimension 0
- req_state: float32 [128, 16, 273, 112], P(('req', 'seq'), 'tp'), parts along dimension 0
- req_norm: float32 [128, 16, 273], P(('req', 'seq'), 'tp'), parts along dimension 0
- req_edge: bfloat16 [128, 2, 1792], P(('req', 'seq'), None, 'tp'), parts along dimension 0
There are 4 independent parts, one for each index of `req`. A program takes and returns all parts, laid end to end along the dimension named above; an argument that names none is the same for every part. Nothing has to cross between parts.
Inputs may be any that keep to these rules, and one draw needn't show every extreme that they name: `prompt_lens`: the lengths sum to 8192, and the largest is half of 8192. `req_group`: every one of the 4 prompts is shared by at least one request. `row_request`: each request appears once; rows i * 4 to (i + 1) * 4 - 1 lie on index i of seq.
All inputs are finite; a program needn't handle non-finite values.
Results may differ from a plain program's by a relative error of at most 0.019.
Values may be sent and summed in bfloat16 or wider, within the bound.
No kernel may reach another device: no remote copies, remote signals or barrier semaphores. Data moves between devices by JAX's collectives and lax.ppermute only.
A program may use at most 64 MiB of HBM per device.

v0:
```python
import jax
import jax.numpy as jnp
from jax import lax
from jax.sharding import PartitionSpec as P

FEAT = 16
HD = 112
KW = 3
PROMPTS = 4
SLOTS = 4
EPS = 1e-05
HIGH = lax.Precision.HIGHEST


def passed_along(shard, axis, by):
    size = lax.axis_size(axis)
    pairs = [(i, i + by) for i in range(size) if 0 <= i + by < size]
    return lax.ppermute(shard, axis, pairs)


def psum_doubling(parts, axis):
    size = lax.axis_size(axis)
    total = [p.astype(jnp.float32) for p in parts]
    step = 1
    while step < size:
        pairs = [(i, i ^ step) for i in range(size)]
        got = lax.ppermute(tuple((t.astype(jnp.bfloat16) for t in total)), axis, pairs)
        total = [t + g.astype(jnp.float32) for t, g in zip(total, got)]
        step *= 2
    return total


def tail_prefix(tail, tail_seg, axis):
    size, here = (lax.axis_size(axis), lax.axis_index(axis))
    seg_before = tail_seg[jnp.maximum(here - 1, 0)]
    group = tail.astype(jnp.float32)
    before = jnp.zeros_like(group)
    step = 1
    while step < size:
        pairs = [(i, i ^ step) for i in range(size)]
        got = lax.ppermute(group.astype(jnp.bfloat16), axis, pairs).astype(jnp.float32)
        other = here ^ step
        my_end = here | step - 1
        other_end = other | step - 1
        same = (tail_seg[my_end] == tail_seg[other_end]).astype(jnp.float32)
        earlier = other < here
        take = (earlier & (tail_seg[other_end] == seg_before)).astype(jnp.float32)
        before = before + take * got
        group = jnp.where(earlier, group + same * got, got + same * group)
        step *= 2
    return before


def taylor_map(values):
    size = values.shape[-1]
    ones = jnp.ones(values.shape[:-1] + (1,), jnp.float32)
    pairs = (values[..., :, None] * values[..., None, :]).reshape(
        values.shape[:-1] + (size * size,)
    )
    return jnp.concatenate([ones, values, pairs * 0.5**0.5], axis=-1)


def segment_ids(positions, ends):
    return jnp.sum((positions[:, None] >= ends[None, :]).astype(jnp.int32), axis=1)


def local(tokens, w_in, conv_w, head_gain, w_out, prompt_lens, req_group, row_request):
    tok_rows = tokens.shape[0]
    width = 2 * FEAT + 2 * HD
    local_heads = w_in.shape[1] // width
    local_cols = local_heads * HD
    seq_pos = lax.axis_index("seq")
    first_row = seq_pos * tok_rows
    ends = jnp.cumsum(prompt_lens)
    starts = ends - prompt_lens
    positions = first_row + jnp.arange(tok_rows, dtype=jnp.int32)
    seg = segment_ids(positions, ends)
    proj = jnp.dot(
        lax.all_gather(tokens, "tp", axis=1, tiled=True), w_in, preferred_element_type=jnp.float32
    )
    proj = proj.astype(jnp.bfloat16).reshape(tok_rows, local_heads, width)
    gate_pre = proj[:, :, 2 * FEAT + HD :].reshape(tok_rows, local_cols)
    rim = passed_along(gate_pre[tok_rows - (KW - 1) :], "seq", 1)
    extended = jnp.concatenate([rim, gate_pre], 0)
    ext_pos = first_row - (KW - 1) + jnp.arange(tok_rows + KW - 1, dtype=jnp.int32)
    ext_seg = segment_ids(ext_pos, ends)
    gate = jnp.zeros((tok_rows, local_cols), jnp.float32)
    for tap in range(KW):
        low = KW - 1 - tap
        same = (ext_seg[low : low + tok_rows] == seg).astype(jnp.float32)
        gate = (
            gate
            + conv_w[tap][None, :]
            * extended[low : low + tok_rows].astype(jnp.float32)
            * same[:, None]
        )
    qs_b = proj[:, :, :FEAT] * jnp.bfloat16(FEAT ** (-0.25))
    ks_b = proj[:, :, FEAT : 2 * FEAT] * jnp.bfloat16(FEAT ** (-0.25))
    qs = qs_b.astype(jnp.float32)
    ks = ks_b.astype(jnp.float32)
    values = proj[:, :, 2 * FEAT : 2 * FEAT + HD]
    values_f = values.astype(jnp.float32)
    dots = jnp.einsum("thf,shf->hts", qs_b, ks_b, preferred_element_type=jnp.float32)
    visible = (positions[None, :] <= positions[:, None]) & (seg[:, None] == seg[None, :])
    weights = jnp.where(visible[None], 1.0 + dots + 0.5 * dots * dots, 0.0)
    numer = jnp.einsum(
        "hts,shd->thd", weights.astype(jnp.bfloat16), values, preferred_element_type=jnp.float32
    )
    phi_q = taylor_map(qs)
    phi_k = taylor_map(ks)
    fmap = phi_k.shape[-1]
    prompt_index = jnp.arange(PROMPTS, dtype=jnp.int32)
    onehot = (seg[:, None] == prompt_index[None, :]).astype(jnp.float32)
    keyed = (onehot[:, :, None, None] * phi_k[:, None, :, :]).reshape(
        tok_rows, PROMPTS * local_heads * fmap
    )
    contrib_state = lax.dot_general(
        keyed.reshape(tok_rows, PROMPTS, local_heads, fmap),
        values_f,
        (((0,), (0,)), ((2,), (1,))),
        precision=HIGH,
    )
    contrib_norm = jnp.einsum("tg,thf->ghf", onehot, phi_k, precision=HIGH)
    offsets = jnp.arange(KW - 1, dtype=jnp.int32)
    edge_rows = ends[:, None] - (KW - 1) + offsets[None, :]
    edge_valid = edge_rows >= starts[:, None]
    match = ((positions[:, None, None] == edge_rows[None]) & edge_valid[None]).astype(jnp.bfloat16)
    contrib_edge = jnp.einsum("tgj,tc->gjc", match, gate_pre, preferred_element_type=jnp.float32)
    block_ends = (jnp.arange(lax.axis_size("seq"), dtype=jnp.int32) + 1) * tok_rows - 1
    tail_seg = segment_ids(block_ends, ends)
    seg_last = tail_seg[seq_pos]
    in_tail = (seg == seg_last).astype(jnp.float32)
    tail_state = jnp.einsum(
        "thf,thd->hfd", phi_k * in_tail[:, None, None], values_f, precision=HIGH
    )
    seg_before = jnp.sum((first_row - 1 >= ends).astype(jnp.int32))
    tails = lax.all_gather(tail_state.astype(jnp.bfloat16), "seq").astype(jnp.float32)
    block_index = jnp.arange(lax.axis_size("seq"), dtype=jnp.int32)
    chained = ((block_index < seq_pos) & (tail_seg == seg_before)).astype(jnp.float32)
    carry_state = jnp.sum(chained.reshape((-1,) + (1,) * (tails.ndim - 1)) * tails, axis=0)
    carried = ((seg == seg_before) & (first_row > 0)).astype(jnp.float32)
    attended = (
        numer
        + jnp.einsum("thf,hfd->thd", phi_q, carry_state, precision=HIGH) * carried[:, None, None]
    )
    inv_rms = lax.rsqrt(jnp.mean(attended * attended, axis=2, keepdims=True) + EPS)
    gain = head_gain.reshape(local_heads, HD)
    hidden = (
        attended * inv_rms * gain[None] * jax.nn.silu(gate.reshape(tok_rows, local_heads, HD))
    ).astype(jnp.bfloat16)
    hidden = hidden.reshape(tok_rows, local_cols)
    product = jnp.einsum(
        "tk,kgc->gtc",
        hidden,
        w_out.reshape(local_cols, lax.axis_size("tp"), -1),
        preferred_element_type=jnp.bfloat16,
    )
    summed = lax.psum_scatter(product, "tp", scatter_dimension=0, tiled=True)
    mixed = summed.reshape(tok_rows, -1)
    all_state, all_norm, all_edge = psum_doubling(
        (contrib_state, contrib_norm, contrib_edge), "seq"
    )
    scale = lax.rsqrt(prompt_lens.astype(jnp.float32))
    my_requests = lax.dynamic_slice_in_dim(row_request, seq_pos * SLOTS, SLOTS)
    my_groups = jnp.take(req_group, my_requests)
    my_scale = jnp.take(scale, my_groups)
    req_state = (
        jnp.take(all_state, my_groups, axis=1).transpose(1, 0, 2, 3) * my_scale[:, None, None, None]
    )
    req_norm = jnp.take(all_norm, my_groups, axis=0) * my_scale[:, None, None]
    req_edge = jnp.take(all_edge, my_groups, axis=0).astype(jnp.bfloat16)
    return (mixed, req_state, req_norm, req_edge)


def solution(mesh):
    in_specs = (
        P(("req", "seq"), "tp"),
        P(None, "tp"),
        P(None, "tp"),
        P("tp"),
        P("tp", None),
        P("req"),
        P("req"),
        P("req"),
    )
    out_specs = (
        P(("req", "seq"), "tp"),
        P(("req", "seq"), "tp", None, None),
        P(("req", "seq"), "tp", None),
        P(("req", "seq"), None, "tp"),
    )
    return jax.shard_map(local, mesh=mesh, in_specs=in_specs, out_specs=out_specs, check_vma=False)
```

profile of v0, /device:TPU:4, one launch (start us, length us, event | category | flops | bytes accessed | tf_op | source)
XLA Modules:
  0.0 200.5 jit_solution(5603790079659906955)
XLA Ops:
  7.2 0.7 all-gather.4.cloned.1.call-update
  8.0 0.8 reduce-window.7
  9.7 1.3 bitcast_subtract_fusion
  11.0 0.6 and_convert_fusion.1
  11.6 0.8 slice_bitcast_fusion.4
  12.4 1.4 fusion.74
  13.8 77.7 %all-gather.4.cloned.1.call-done = bf16[1024,1792]{0,1:T(8,128)(2,1)} async-done(((bf16[1024,112]{0,1:T(8,128)(2,1)}), bf16[1024,1792]{0,1:T(8,128)(2,1)}) %all-gather.4.cloned.1.call-update) | async-done | bytes 3670032 | tf_op jit(solution)/shard_map/all_gather | solution.py:79
  91.5 3.2 %fusion.8 = bf16[1024,1,256]{0,2,1:T(8,128)(2,1)S(1)} fusion(bf16[1024,1792]{0,1:T(8,128)(2,1)} %all-gather.4.cloned.1.call-done, bf16[1792,256]{1,0:T(8,128)(2,1)S(1)} %copy-done), kind=kOutput, calls=%fused_computation.15 | convolution fusion | flops 939786240 | bytes 5111808 | tf_op jit(solution)/shard_map/dot_general | solution.py:78
  94.8 1.7 fusion.9
  96.5 1.9 collective-permute-start
  98.7 0.8 fusion.25
  99.5 12.1 %all-gather.1 = bf16[8,273,112]{2,1,0:T(8,128)(2,1)S(1)} all-gather(bf16[1,273,112]{2,1,0:T(8,128)(2,1)S(1)} %fusion.25), channel_id=2, replica_groups=mesh['seq'=8,'tp'=16,'req'=4] {'seq'}, dimensions={0}, use_global_device_ids=true | all-gather | bytes 550368 | tf_op jit(solution)/shard_map/all_gather | solution.py:137
  111.9 1.2 multiply_reduce_fusion
  113.2 3.2 %fusion.38 = bf16[1024,1792]{0,1} fusion(bf16[112,1792]{1,0:T(8,128)(2,1)S(1)} %copy-done.2, bf16[1024,112]{0,1:T(8,128)(2,1)S(1)} %slice_bitcast_fusion, f32[1,112,1024]{2,1,0:T(8,128)S(1)} %get-tuple-element.39, bf16[2,112]{0,1:T(8,128)(2,1)S(1)} %collective-permute-done, f32[1024]{0:T(1024)S(1)} %get-tuple-element.28, f32[112]{0:T(128)S(1)} %get-tuple-element.33, ...), kind=kOutput, calls=%fused_computation.57 | convolution fusion | flops 413908992 | bytes 4778176
  117.1 0.6 gather_fusion
  117.8 0.6 gather_fusion.2
  118.7 2.3 %collective-permute-start.7 = (bf16[4,2,112]{2,0,1:T(4,128)(2,1)S(1)}, bf16[4,2,112]{2,0,1:T(4,128)(2,1)S(1)}, u32[]{:S(2)}, u32[]{:S(2)}) collective-permute-start(bf16[4,2,112]{2,0,1:T(4,128)(2,1)S(1)} %get-tuple-element.40), channel_id=1, source_target_pairs={{0,64},{64,0},{128,192},{192,128},{256,320},{320,256},{384,448},{4... | collective-permute-start | bytes 5384 | tf_op jit(solution)/shard_map/ppermute | solution.py:27
  121.0 0.8 fusion.65
  121.8 2.1 %collective-permute-start.4 = (bf16[4,1,273]{2,0,1:T(4,128)(2,1)S(1)}, bf16[4,1,273]{2,0,1:T(4,128)(2,1)S(1)}, u32[]{:S(2)}, u32[]{:S(2)}) collective-permute-start(bf16[4,1,273]{2,0,1:T(4,128)(2,1)S(1)} %convert_bitcast_fusion.3), channel_id=1, source_target_pairs={{0,64},{64,0},{128,192},{192,128},{256,320},{320,256},{384,448},{4... | collective-permute-start | bytes 6560 | tf_op jit(solution)/shard_map/ppermute | solution.py:27
  124.0 2.3 %fusion = f32[4,273,112]{2,1,0:T(8,128)S(1)} fusion(f32[1024,273]{0,1:T(8,128)S(1)} %maximum_bitcast_fusion.2, f32[1024,4]{0,1:T(4,128)S(1)} %fusion.66, bf16[1024,1,256]{0,2,1:T(8,128)(2,1)S(1)} %fusion.8), kind=kOutput, calls=%fused_computation.6 | convolution fusion | flops 1503989760 | bytes 1881856 | tf_op jit(solution)/shard_map/dot_general | solution.py:117
  126.4 2.3 %collective-permute-start.1 = (bf16[1,4,273,112]{3,2,1,0:T(8,128)(2,1)S(1)}, bf16[1,4,273,112]{3,2,1,0:T(8,128)(2,1)S(1)}, u32[]{:S(2)}, u32[]{:S(2)}) collective-permute-start(bf16[1,4,273,112]{3,2,1,0:T(8,128)(2,1)S(1)} %convert_bitcast_fusion), channel_id=1, source_target_pairs={{0,64},{64,0},{128,192},{192,128},{256,320},{320,256},{384,448},{4... | collective-permute-start | bytes 733832 | tf_op jit(solution)/shard_map/ppermute | solution.py:27
  128.7 4.1 %collective-permute-start.8 = (bf16[4,2,112]{2,0,1:T(4,128)(2,1)S(1)}, bf16[4,2,112]{2,0,1:T(4,128)(2,1)S(1)}, u32[]{:S(2)}, u32[]{:S(2)}) collective-permute-start(bf16[4,2,112]{2,0,1:T(4,128)(2,1)S(1)} %fusion.78), channel_id=1, source_target_pairs={{0,128},{64,192},{128,0},{192,64},{256,384},{320,448},{384,256},{4... | collective-permute-start | bytes 5384 | tf_op jit(solution)/shard_map/ppermute | solution.py:27
  132.9 1.9 collective-permute-start.5
  134.8 3.8 %collective-permute-start.9 = (bf16[4,2,112]{2,0,1:T(4,128)(2,1)S(1)}, bf16[4,2,112]{2,0,1:T(4,128)(2,1)S(1)}, u32[]{:S(2)}, u32[]{:S(2)}) collective-permute-start(bf16[4,2,112]{2,0,1:T(4,128)(2,1)S(1)} %fusion.80), channel_id=1, source_target_pairs={{0,256},{64,320},{128,384},{192,448},{256,0},{320,64},{384,128},{4... | collective-permute-start | bytes 5384 | tf_op jit(solution)/shard_map/ppermute | solution.py:27
  138.7 3.6 %collective-permute-start.6 = (bf16[4,1,273]{2,0,1:T(4,128)(2,1)S(1)}, bf16[4,1,273]{2,0,1:T(4,128)(2,1)S(1)}, u32[]{:S(2)}, u32[]{:S(2)}) collective-permute-start(bf16[4,1,273]{2,0,1:T(4,128)(2,1)S(1)} %fusion.77), channel_id=1, source_target_pairs={{0,256},{64,320},{128,384},{192,448},{256,0},{320,64},{384,128},{4... | collective-permute-start | bytes 6560 | tf_op jit(solution)/shard_map/ppermute | solution.py:27
  142.3 3.9 %collective-permute-start.2 = (bf16[1,4,273,112]{3,2,1,0:T(8,128)(2,1)S(1)}, bf16[1,4,273,112]{3,2,1,0:T(8,128)(2,1)S(1)}, u32[]{:S(2)}, u32[]{:S(2)}) collective-permute-start(bf16[1,4,273,112]{3,2,1,0:T(8,128)(2,1)S(1)} %fusion.51), channel_id=1, source_target_pairs={{0,128},{64,192},{128,0},{192,64},{256,384},{320,448},{384,256},{4... | collective-permute-start | bytes 733832 | tf_op jit(solution)/shard_map/ppermute | solution.py:27
  146.8 0.7 select_convert_fusion
  147.5 4.8 %collective-permute-done.2 = bf16[1,4,273,112]{3,2,1,0:T(8,128)(2,1)S(1)} collective-permute-done((bf16[1,4,273,112]{3,2,1,0:T(8,128)(2,1)S(1)}, bf16[1,4,273,112]{3,2,1,0:T(8,128)(2,1)S(1)}, u32[]{:S(2)}, u32[]{:S(2)}) %collective-permute-start.2) | collective-permute-done | bytes 244640 | tf_op jit(solution)/shard_map/ppermute | solution.py:27
  152.4 3.5 %collective-permute-start.3 = (bf16[1,4,273,112]{3,2,1,0:T(8,128)(2,1)S(1)}, bf16[1,4,273,112]{3,2,1,0:T(8,128)(2,1)S(1)}, u32[]{:S(2)}, u32[]{:S(2)}) collective-permute-start(bf16[1,4,273,112]{3,2,1,0:T(8,128)(2,1)S(1)} %fusion.33), channel_id=1, source_target_pairs={{0,256},{64,320},{128,384},{192,448},{256,0},{320,64},{384,128},{4... | collective-permute-start | bytes 733832 | tf_op jit(solution)/shard_map/ppermute | solution.py:27
  157.2 5.9 %collective-permute-done.3 = bf16[1,4,273,112]{3,2,1,0:T(8,128)(2,1)S(1)} collective-permute-done((bf16[1,4,273,112]{3,2,1,0:T(8,128)(2,1)S(1)}, bf16[1,4,273,112]{3,2,1,0:T(8,128)(2,1)S(1)}, u32[]{:S(2)}, u32[]{:S(2)}) %collective-permute-start.3) | collective-permute-done | bytes 244640 | tf_op jit(solution)/shard_map/ppermute | solution.py:27
  163.9 1.4 copy.26
  165.3 28.3 %reduce-scatter.2.cloned.1.call-done = bf16[1,1024,112]{1,2,0:T(8,128)(2,1)} async-done(((bf16[16,1024,112]{1,2,0:T(8,128)(2,1)}), bf16[1,1024,112]{1,2,0:T(8,128)(2,1)}) %reduce-scatter.2.cloned.1.call-update) | async-done | bytes 229392 | tf_op jit(solution)/shard_map/reduce_scatter | solution.py:158
  (67 shorter events, 5.7 us)
Async XLA Ops:
  7.2 84.3 %copy-start = (bf16[1792,256]{1,0:T(8,128)(2,1)S(1)}, bf16[1792,256]{1,0:T(8,128)(2,1)}, u32[]{:S(2)}) copy-start(bf16[1792,256]{1,0:T(8,128)(2,1)} %param.9) | copy-start | bytes 2752516
  7.2 84.3 %all-gather.4.cloned.1.call-start = ((), (), s32[]{:S(2)}) async-start(), calls=%async_computation.1 | async-start | bytes 3899392 | tf_op jit(solution)/shard_map/all_gather | solution.py:79
  7.9 185.8 %reduce-scatter.2.cloned.1.call-start = ((), (), s32[]{:S(2)}) async-start(), calls=%async_computation.2 | async-start | bytes 3899392 | tf_op jit(solution)/shard_map/reduce_scatter | solution.py:158
  96.5 16.6 %collective-permute-start = (bf16[2,112]{0,1:T(8,128)(2,1)S(1)}, bf16[2,112]{0,1:T(8,128)(2,1)S(1)}, u32[]{:S(2)}, u32[]{:S(2)}) collective-permute-start(bf16[2,112]{0,1:T(8,128)(2,1)S(1)} %slice_bitcast_fusion.1), channel_id=1, source_target_pairs={{0,64},{64,128},{128,192},{192,256},{256,320},{320,384},{384,448},... | collective-permute-start | bytes 1352 | tf_op jit(solution)/shard_map/ppermute | solution.py:18
  111.9 1.3 copy-start.2
  111.9 1.3 copy-start.3
  116.3 0.7 copy-start.4
  116.3 0.7 copy-start.1
  116.3 1.5 copy-start.5
  118.7 10.0 %collective-permute-start.7 = (bf16[4,2,112]{2,0,1:T(4,128)(2,1)S(1)}, bf16[4,2,112]{2,0,1:T(4,128)(2,1)S(1)}, u32[]{:S(2)}, u32[]{:S(2)}) collective-permute-start(bf16[4,2,112]{2,0,1:T(4,128)(2,1)S(1)} %get-tuple-element.40), channel_id=1, source_target_pairs={{0,64},{64,0},{128,192},{192,128},{256,320},{320,256},{384,448},{4... | collective-permute-start | bytes 5384 | tf_op jit(solution)/shard_map/ppermute | solution.py:27
  121.8 11.1 %collective-permute-start.4 = (bf16[4,1,273]{2,0,1:T(4,128)(2,1)S(1)}, bf16[4,1,273]{2,0,1:T(4,128)(2,1)S(1)}, u32[]{:S(2)}, u32[]{:S(2)}) collective-permute-start(bf16[4,1,273]{2,0,1:T(4,128)(2,1)S(1)} %convert_bitcast_fusion.3), channel_id=1, source_target_pairs={{0,64},{64,0},{128,192},{192,128},{256,320},{320,256},{384,448},{4... | collective-permute-start | bytes 6560 | tf_op jit(solution)/shard_map/ppermute | solution.py:27
  126.4 15.8 %collective-permute-start.1 = (bf16[1,4,273,112]{3,2,1,0:T(8,128)(2,1)S(1)}, bf16[1,4,273,112]{3,2,1,0:T(8,128)(2,1)S(1)}, u32[]{:S(2)}, u32[]{:S(2)}) collective-permute-start(bf16[1,4,273,112]{3,2,1,0:T(8,128)(2,1)S(1)} %convert_bitcast_fusion), channel_id=1, source_target_pairs={{0,64},{64,0},{128,192},{192,128},{256,320},{320,256},{384,448},{4... | collective-permute-start | bytes 733832 | tf_op jit(solution)/shard_map/ppermute | solution.py:27
  128.7 6.1 %collective-permute-start.8 = (bf16[4,2,112]{2,0,1:T(4,128)(2,1)S(1)}, bf16[4,2,112]{2,0,1:T(4,128)(2,1)S(1)}, u32[]{:S(2)}, u32[]{:S(2)}) collective-permute-start(bf16[4,2,112]{2,0,1:T(4,128)(2,1)S(1)} %fusion.78), channel_id=1, source_target_pairs={{0,128},{64,192},{128,0},{192,64},{256,384},{320,448},{384,256},{4... | collective-permute-start | bytes 5384 | tf_op jit(solution)/shard_map/ppermute | solution.py:27
  132.9 5.7 %collective-permute-start.5 = (bf16[4,1,273]{2,0,1:T(4,128)(2,1)S(1)}, bf16[4,1,273]{2,0,1:T(4,128)(2,1)S(1)}, u32[]{:S(2)}, u32[]{:S(2)}) collective-permute-start(bf16[4,1,273]{2,0,1:T(4,128)(2,1)S(1)} %fusion.79), channel_id=1, source_target_pairs={{0,128},{64,192},{128,0},{192,64},{256,384},{320,448},{384,256},{4... | collective-permute-start | bytes 6560 | tf_op jit(solution)/shard_map/ppermute | solution.py:27
  134.8 11.4 %collective-permute-start.9 = (bf16[4,2,112]{2,0,1:T(4,128)(2,1)S(1)}, bf16[4,2,112]{2,0,1:T(4,128)(2,1)S(1)}, u32[]{:S(2)}, u32[]{:S(2)}) collective-permute-start(bf16[4,2,112]{2,0,1:T(4,128)(2,1)S(1)} %fusion.80), channel_id=1, source_target_pairs={{0,256},{64,320},{128,384},{192,448},{256,0},{320,64},{384,128},{4... | collective-permute-start | bytes 5384 | tf_op jit(solution)/shard_map/ppermute | solution.py:27
  138.7 17.2 %collective-permute-start.6 = (bf16[4,1,273]{2,0,1:T(4,128)(2,1)S(1)}, bf16[4,1,273]{2,0,1:T(4,128)(2,1)S(1)}, u32[]{:S(2)}, u32[]{:S(2)}) collective-permute-start(bf16[4,1,273]{2,0,1:T(4,128)(2,1)S(1)} %fusion.77), channel_id=1, source_target_pairs={{0,256},{64,320},{128,384},{192,448},{256,0},{320,64},{384,128},{4... | collective-permute-start | bytes 6560 | tf_op jit(solution)/shard_map/ppermute | solution.py:27
  142.3 10.0 %collective-permute-start.2 = (bf16[1,4,273,112]{3,2,1,0:T(8,128)(2,1)S(1)}, bf16[1,4,273,112]{3,2,1,0:T(8,128)(2,1)S(1)}, u32[]{:S(2)}, u32[]{:S(2)}) collective-permute-start(bf16[1,4,273,112]{3,2,1,0:T(8,128)(2,1)S(1)} %fusion.51), channel_id=1, source_target_pairs={{0,128},{64,192},{128,0},{192,64},{256,384},{320,448},{384,256},{4... | collective-permute-start | bytes 733832 | tf_op jit(solution)/shard_map/ppermute | solution.py:27
  152.4 10.7 %collective-permute-start.3 = (bf16[1,4,273,112]{3,2,1,0:T(8,128)(2,1)S(1)}, bf16[1,4,273,112]{3,2,1,0:T(8,128)(2,1)S(1)}, u32[]{:S(2)}, u32[]{:S(2)}) collective-permute-start(bf16[1,4,273,112]{3,2,1,0:T(8,128)(2,1)S(1)} %fusion.33), channel_id=1, source_target_pairs={{0,256},{64,320},{128,384},{192,448},{256,0},{320,64},{384,128},{4... | collective-permute-start | bytes 733832 | tf_op jit(solution)/shard_map/ppermute | solution.py:27
Sparse Core Ops, SparseCore 0:
  10.1 81.3 all-gather.3
  116.5 77.1 reduce-scatter.1
where the time goes:
time: 201 us
  waiting for transfers between devices  117 us (58%)
  starting transfers between devices  29.5 us (15%)
  between operations  14.5 us (7%)
  matrix products  13.4 us (7%)
  blocking collectives  12.1 us (6%)
  local copies, waits for them, and re-layouts  7.13 us (4%)
  other arithmetic  6.52 us (3%)
    all_gather x1, waiting for transfers between devices, local(): lax.all_gather(tokens, 'tp', axis=1, tiled=True)  77.7 us
    reduce_scatter x1, waiting for transfers between devices, local(): summed = lax.psum_scatter(product, 'tp', scatter_dimension=0, tiled=True)  28.3 us
    ppermute x9, starting transfers between devices, psum_doubling(): lax.ppermute(tuple((t.astype(jnp.bfloat16) for t in total)), axis, pairs)  27.5 us
    all_gather x1, blocking collectives, local(): lax.all_gather(tail_state.astype(jnp.bfloat16), 'seq').astype(jnp.float32)  12.1 us
    ppermute x9, waiting for transfers between devices, psum_doubling(): lax.ppermute(tuple((t.astype(jnp.bfloat16) for t in total)), axis, pairs)  10.7 us
  transfers between devices with their start and end apart: 12, of which 4 were waited for; matrix products, arithmetic and copies ran while one was open for 9% of the time, Pallas kernels for 0%

commit v1 on v0

--- a/solution.py
+++ b/solution.py
@@ -2,6 +2,7 @@
 import jax.numpy as jnp
 from jax import lax
 from jax.sharding import PartitionSpec as P
+from jax.lax import all_to_all, axis_size
 
 FEAT = 16
 HD = 112
@@ -76,7 +77,11 @@
     positions = first_row + jnp.arange(tok_rows, dtype=jnp.int32)
     seg = segment_ids(positions, ends)
     proj = jnp.dot(
-        lax.all_gather(tokens, "tp", axis=1, tiled=True), w_in, preferred_element_type=jnp.float32
+        jnp.concatenate(
+            all_to_all(jnp.stack([tokens for _ in range(axis_size("tp"))]), "tp", 0, 0), 1
+        ),
+        w_in,
+        preferred_element_type=jnp.float32,
     )
     proj = proj.astype(jnp.bfloat16).reshape(tok_rows, local_heads, width)
     gate_pre = proj[:, :, 2 * FEAT + HD :].reshape(tok_rows, local_cols)

time: 201 us -> 301 us (1.50)
  the two profiles are of different devices: /device:TPU:4 before, /device:TPU:20 now
where the time goes in v1:
time: 301 us; the launch traced here: 300 us
  waiting for transfers between devices  200 us (66%)
  starting transfers between devices  44.1 us (15%)
  between operations  14.4 us (5%)
  matrix products  14.3 us (5%)
  blocking collectives  12 us (4%)
  local copies, waits for them, and re-layouts  10.5 us (3%)
  other arithmetic  5.18 us (2%)
    all_to_all x1, waiting for transfers between devices, local(): all_to_all(jnp.stack([tokens for _ in range(axis_size('tp'))]), 'tp', 0, 0)  156 us
    reduce_scatter x1, waiting for transfers between devices, local(): summed = lax.psum_scatter(product, 'tp', scatter_dimension=0, tiled=True)  30.1 us
    ppermute x9, starting transfers between devices, psum_doubling(): lax.ppermute(tuple((t.astype(jnp.bfloat16) for t in total)), axis, pairs)  26.4 us
    all_to_all x1, starting transfers between devices, local(): all_to_all(jnp.stack([tokens for _ in range(axis_size('tp'))]), 'tp', 0, 0)  15.4 us
    all_gather x1, blocking collectives, local(): lax.all_gather(tail_state.astype(jnp.bfloat16), 'seq').astype(jnp.float32)  12 us
    ppermute x9, waiting for transfers between devices, psum_doubling(): lax.ppermute(tuple((t.astype(jnp.bfloat16) for t in total)), axis, pairs)  11.9 us
  transfers between devices with their start and end apart: 12, of which 6 were waited for; matrix products, arithmetic and copies ran while one was open for 5% of the time, Pallas kernels for 0%

profile of v1, /device:TPU:20, one launch (start us, length us, event | category | flops | bytes accessed | tf_op | source)
XLA Modules:
  0.0 300.1 jit_solution(6153945361135634518)
XLA Ops:
  7.2 3.3 %stack.2 = bf16[16,1024,112]{1,2,0:T(8,128)(2,1)} broadcast(bf16[1024,112]{0,1:T(8,128)(2,1)} %param.8), dimensions={1,2} | broadcast | bytes 3899392 | tf_op jit(solution)/shard_map/stack | solution.py:81
  10.5 15.4 %all-to-all-start = ((bf16[16,1024,112]{1,2,0:T(8,128)(2,1)}), bf16[16,1024,112]{1,2,0:T(8,128)(2,1)}, u32[]{:S(2)}, u32[]{:S(2)}) async-start(bf16[16,1024,112]{1,2,0:T(8,128)(2,1)} %stack.2), calls=%async_computation | async-start | bytes 7340032 | tf_op jit(solution)/shard_map/all_to_all | solution.py:81
  27.6 0.6 and_convert_fusion.1
  28.3 1.4 fusion.74
  29.7 156.1 %all-to-all-done = bf16[16,1024,112]{1,2,0:T(8,128)(2,1)} async-done(((bf16[16,1024,112]{1,2,0:T(8,128)(2,1)}), bf16[16,1024,112]{1,2,0:T(8,128)(2,1)}, u32[]{:S(2)}, u32[]{:S(2)}) %all-to-all-start) | async-done | bytes 3670048 | tf_op jit(solution)/shard_map/all_to_all | solution.py:81
  185.7 3.2 %fusion.8 = bf16[1024,1,256]{0,2,1:T(8,128)(2,1)S(1)} fusion(bf16[1024,1792]{0,1:T(8,128)(2,1)} %bitcast.1, bf16[1792,256]{1,0:T(8,128)(2,1)S(1)} %copy-done), kind=kOutput, calls=%fused_computation.15 | convolution fusion | flops 939786240 | bytes 5111808 | tf_op jit(solution)/shard_map/dot_general | solution.py:79
  189.0 1.7 fusion.9
  190.9 1.8 fusion.25
  192.7 12.0 %all-gather.1 = bf16[8,273,112]{2,1,0:T(8,128)(2,1)S(1)} all-gather(bf16[1,273,112]{2,1,0:T(8,128)(2,1)S(1)} %fusion.25), channel_id=2, replica_groups=mesh['seq'=8,'tp'=16,'req'=4] {'seq'}, dimensions={0}, use_global_device_ids=true | all-gather | bytes 550368 | tf_op jit(solution)/shard_map/all_gather | solution.py:142
  204.8 2.3 collective-permute-start
  207.3 1.2 multiply_reduce_fusion
  208.6 1.5 collective-permute-done
  210.0 3.2 %fusion.38 = bf16[1024,1792]{0,1} fusion(bf16[112,1792]{1,0:T(8,128)(2,1)S(1)} %copy-done.2, bf16[1024,112]{0,1:T(8,128)(2,1)S(1)} %slice_bitcast_fusion, f32[1,112,1024]{2,1,0:T(8,128)S(1)} %get-tuple-element.39, bf16[2,112]{0,1:T(8,128)(2,1)S(1)} %collective-permute-done, f32[1024]{0:T(1024)S(1)} %get-tuple-element.28, f32[112]{0:T(128)S(1)} %get-tuple-element.33, ...), kind=kOutput, calls=%fused_computation.57 | convolution fusion | flops 413908992 | bytes 4778176
  213.9 0.6 gather_fusion
  214.7 0.6 gather_fusion.2
  215.5 0.9 copy-done.4
  216.4 2.3 fusion
  218.8 2.7 collective-permute-start.1
  221.6 1.9 collective-permute-start.7
  223.6 0.8 fusion.65
  224.3 2.4 collective-permute-start.4
  226.8 3.6 %collective-permute-start.8 = (bf16[4,2,112]{2,0,1:T(4,128)(2,1)S(1)}, bf16[4,2,112]{2,0,1:T(4,128)(2,1)S(1)}, u32[]{:S(2)}, u32[]{:S(2)}) collective-permute-start(bf16[4,2,112]{2,0,1:T(4,128)(2,1)S(1)} %fusion.78), channel_id=1, source_target_pairs={{0,128},{64,192},{128,0},{192,64},{256,384},{320,448},{384,256},{4... | collective-permute-start | bytes 5384 | tf_op jit(solution)/shard_map/ppermute | solution.py:28
  230.4 2.3 collective-permute-start.5
  232.7 2.8 collective-permute-start.9
  235.9 4.2 %collective-permute-start.6 = (bf16[4,1,273]{2,0,1:T(4,128)(2,1)S(1)}, bf16[4,1,273]{2,0,1:T(4,128)(2,1)S(1)}, u32[]{:S(2)}, u32[]{:S(2)}) collective-permute-start(bf16[4,1,273]{2,0,1:T(4,128)(2,1)S(1)} %fusion.77), channel_id=1, source_target_pairs={{0,256},{64,320},{128,384},{192,448},{256,0},{320,64},{384,128},{4... | collective-permute-start | bytes 6560 | tf_op jit(solution)/shard_map/ppermute | solution.py:28
  240.2 3.6 %collective-permute-start.2 = (bf16[1,4,273,112]{3,2,1,0:T(8,128)(2,1)S(1)}, bf16[1,4,273,112]{3,2,1,0:T(8,128)(2,1)S(1)}, u32[]{:S(2)}, u32[]{:S(2)}) collective-permute-start(bf16[1,4,273,112]{3,2,1,0:T(8,128)(2,1)S(1)} %fusion.51), channel_id=1, source_target_pairs={{0,128},{64,192},{128,0},{192,64},{256,384},{320,448},{384,256},{4... | collective-permute-start | bytes 733832 | tf_op jit(solution)/shard_map/ppermute | solution.py:28
  244.4 0.7 select_convert_fusion
  245.0 5.1 %collective-permute-done.2 = bf16[1,4,273,112]{3,2,1,0:T(8,128)(2,1)S(1)} collective-permute-done((bf16[1,4,273,112]{3,2,1,0:T(8,128)(2,1)S(1)}, bf16[1,4,273,112]{3,2,1,0:T(8,128)(2,1)S(1)}, u32[]{:S(2)}, u32[]{:S(2)}) %collective-permute-start.2) | collective-permute-done | bytes 244640 | tf_op jit(solution)/shard_map/ppermute | solution.py:28
  250.2 3.0 %collective-permute-start.3 = (bf16[1,4,273,112]{3,2,1,0:T(8,128)(2,1)S(1)}, bf16[1,4,273,112]{3,2,1,0:T(8,128)(2,1)S(1)}, u32[]{:S(2)}, u32[]{:S(2)}) collective-permute-start(bf16[1,4,273,112]{3,2,1,0:T(8,128)(2,1)S(1)} %fusion.33), channel_id=1, source_target_pairs={{0,256},{64,320},{128,384},{192,448},{256,0},{320,64},{384,128},{4... | collective-permute-start | bytes 733832 | tf_op jit(solution)/shard_map/ppermute | solution.py:28
  254.5 6.4 %collective-permute-done.3 = bf16[1,4,273,112]{3,2,1,0:T(8,128)(2,1)S(1)} collective-permute-done((bf16[1,4,273,112]{3,2,1,0:T(8,128)(2,1)S(1)}, bf16[1,4,273,112]{3,2,1,0:T(8,128)(2,1)S(1)}, u32[]{:S(2)}, u32[]{:S(2)}) %collective-permute-start.3) | collective-permute-done | bytes 244640 | tf_op jit(solution)/shard_map/ppermute | solution.py:28
  261.7 1.4 copy.27
  263.1 30.1 %reduce-scatter.2.cloned.1.call-done = bf16[1,1024,112]{1,2,0:T(8,128)(2,1)} async-done(((bf16[16,1024,112]{1,2,0:T(8,128)(2,1)}), bf16[1,1024,112]{1,2,0:T(8,128)(2,1)}) %reduce-scatter.2.cloned.1.call-update) | async-done | bytes 229392 | tf_op jit(solution)/shard_map/reduce_scatter | solution.py:163
  (73 shorter events, 6.9 us)
Async XLA Ops:
  7.2 178.6 %copy-start = (bf16[1792,256]{1,0:T(8,128)(2,1)S(1)}, bf16[1792,256]{1,0:T(8,128)(2,1)}, u32[]{:S(2)}) copy-start(bf16[1792,256]{1,0:T(8,128)(2,1)} %param.9) | copy-start | bytes 2752516
  10.5 15.4 %copy-start.8 = (s32[4]{0:T(128)S(1)}, s32[4]{0:T(128)}, u32[]{:S(2)}) copy-start(s32[4]{0:T(128)} %param.13) | copy-start | bytes 52
  10.5 17.8 %copy-start.5 = (f32[3,112]{1,0:T(4,128)S(1)}, f32[3,112]{1,0:T(4,128)}, u32[]{:S(2)}) copy-start(f32[3,112]{1,0:T(4,128)} %param.10) | copy-start | bytes 4036
  10.5 175.2 %all-to-all-start = ((bf16[16,1024,112]{1,2,0:T(8,128)(2,1)}), bf16[16,1024,112]{1,2,0:T(8,128)(2,1)}, u32[]{:S(2)}, u32[]{:S(2)}) async-start(bf16[16,1024,112]{1,2,0:T(8,128)(2,1)} %stack.2), calls=%async_computation | async-start | bytes 7340032 | tf_op jit(solution)/shard_map/all_to_all | solution.py:81
  25.9 267.4 %reduce-scatter.2.cloned.1.call-start = ((), (), s32[]{:S(2)}) async-start(), calls=%async_computation.2 | async-start | bytes 3899392 | tf_op jit(solution)/shard_map/reduce_scatter | solution.py:163
  188.9 1.8 copy-start.3
  204.8 5.2 %collective-permute-start = (bf16[2,112]{0,1:T(8,128)(2,1)S(1)}, bf16[2,112]{0,1:T(8,128)(2,1)S(1)}, u32[]{:S(2)}, u32[]{:S(2)}) collective-permute-start(bf16[2,112]{0,1:T(8,128)(2,1)S(1)} %slice_bitcast_fusion.1), channel_id=1, source_target_pairs={{0,64},{64,128},{128,192},{192,256},{256,320},{320,384},{384,448},... | collective-permute-start | bytes 1352 | tf_op jit(solution)/shard_map/ppermute | solution.py:19
  207.3 2.7 copy-start.2
  207.3 2.7 copy-start.6
  213.2 0.7 copy-start.7
  213.2 0.7 copy-start.1
  215.3 1.0 copy-start.4
  218.8 21.3 %collective-permute-start.1 = (bf16[1,4,273,112]{3,2,1,0:T(8,128)(2,1)S(1)}, bf16[1,4,273,112]{3,2,1,0:T(8,128)(2,1)S(1)}, u32[]{:S(2)}, u32[]{:S(2)}) collective-permute-start(bf16[1,4,273,112]{3,2,1,0:T(8,128)(2,1)S(1)} %convert_bitcast_fusion), channel_id=1, source_target_pairs={{0,64},{64,0},{128,192},{192,128},{256,320},{320,256},{384,448},{4... | collective-permute-start | bytes 733832 | tf_op jit(solution)/shard_map/ppermute | solution.py:28
  221.6 5.2 %collective-permute-start.7 = (bf16[4,2,112]{2,0,1:T(4,128)(2,1)S(1)}, bf16[4,2,112]{2,0,1:T(4,128)(2,1)S(1)}, u32[]{:S(2)}, u32[]{:S(2)}) collective-permute-start(bf16[4,2,112]{2,0,1:T(4,128)(2,1)S(1)} %get-tuple-element.40), channel_id=1, source_target_pairs={{0,64},{64,0},{128,192},{192,128},{256,320},{320,256},{384,448},{4... | collective-permute-start | bytes 5384 | tf_op jit(solution)/shard_map/ppermute | solution.py:28
  224.3 6.0 %collective-permute-start.4 = (bf16[4,1,273]{2,0,1:T(4,128)(2,1)S(1)}, bf16[4,1,273]{2,0,1:T(4,128)(2,1)S(1)}, u32[]{:S(2)}, u32[]{:S(2)}) collective-permute-start(bf16[4,1,273]{2,0,1:T(4,128)(2,1)S(1)} %convert_bitcast_fusion.3), channel_id=1, source_target_pairs={{0,64},{64,0},{128,192},{192,128},{256,320},{320,256},{384,448},{4... | collective-permute-start | bytes 6560 | tf_op jit(solution)/shard_map/ppermute | solution.py:28
  226.8 5.9 %collective-permute-start.8 = (bf16[4,2,112]{2,0,1:T(4,128)(2,1)S(1)}, bf16[4,2,112]{2,0,1:T(4,128)(2,1)S(1)}, u32[]{:S(2)}, u32[]{:S(2)}) collective-permute-start(bf16[4,2,112]{2,0,1:T(4,128)(2,1)S(1)} %fusion.78), channel_id=1, source_target_pairs={{0,128},{64,192},{128,0},{192,64},{256,384},{320,448},{384,256},{4... | collective-permute-start | bytes 5384 | tf_op jit(solution)/shard_map/ppermute | solution.py:28
  230.4 5.5 %collective-permute-start.5 = (bf16[4,1,273]{2,0,1:T(4,128)(2,1)S(1)}, bf16[4,1,273]{2,0,1:T(4,128)(2,1)S(1)}, u32[]{:S(2)}, u32[]{:S(2)}) collective-permute-start(bf16[4,1,273]{2,0,1:T(4,128)(2,1)S(1)} %fusion.79), channel_id=1, source_target_pairs={{0,128},{64,192},{128,0},{192,64},{256,384},{320,448},{384,256},{4... | collective-permute-start | bytes 6560 | tf_op jit(solution)/shard_map/ppermute | solution.py:28
  232.7 11.0 %collective-permute-start.9 = (bf16[4,2,112]{2,0,1:T(4,128)(2,1)S(1)}, bf16[4,2,112]{2,0,1:T(4,128)(2,1)S(1)}, u32[]{:S(2)}, u32[]{:S(2)}) collective-permute-start(bf16[4,2,112]{2,0,1:T(4,128)(2,1)S(1)} %fusion.80), channel_id=1, source_target_pairs={{0,256},{64,320},{128,384},{192,448},{256,0},{320,64},{384,128},{4... | collective-permute-start | bytes 5384 | tf_op jit(solution)/shard_map/ppermute | solution.py:28
  235.9 17.4 %collective-permute-start.6 = (bf16[4,1,273]{2,0,1:T(4,128)(2,1)S(1)}, bf16[4,1,273]{2,0,1:T(4,128)(2,1)S(1)}, u32[]{:S(2)}, u32[]{:S(2)}) collective-permute-start(bf16[4,1,273]{2,0,1:T(4,128)(2,1)S(1)} %fusion.77), channel_id=1, source_target_pairs={{0,256},{64,320},{128,384},{192,448},{256,0},{320,64},{384,128},{4... | collective-permute-start | bytes 6560 | tf_op jit(solution)/shard_map/ppermute | solution.py:28
  240.2 9.9 %collective-permute-start.2 = (bf16[1,4,273,112]{3,2,1,0:T(8,128)(2,1)S(1)}, bf16[1,4,273,112]{3,2,1,0:T(8,128)(2,1)S(1)}, u32[]{:S(2)}, u32[]{:S(2)}) collective-permute-start(bf16[1,4,273,112]{3,2,1,0:T(8,128)(2,1)S(1)} %fusion.51), channel_id=1, source_target_pairs={{0,128},{64,192},{128,0},{192,64},{256,384},{320,448},{384,256},{4... | collective-permute-start | bytes 733832 | tf_op jit(solution)/shard_map/ppermute | solution.py:28
  250.2 10.7 %collective-permute-start.3 = (bf16[1,4,273,112]{3,2,1,0:T(8,128)(2,1)S(1)}, bf16[1,4,273,112]{3,2,1,0:T(8,128)(2,1)S(1)}, u32[]{:S(2)}, u32[]{:S(2)}) collective-permute-start(bf16[1,4,273,112]{3,2,1,0:T(8,128)(2,1)S(1)} %fusion.33), channel_id=1, source_target_pairs={{0,256},{64,320},{128,384},{192,448},{256,0},{320,64},{384,128},{4... | collective-permute-start | bytes 733832 | tf_op jit(solution)/shard_map/ppermute | solution.py:28
Sparse Core Ops, SparseCore 0:
  213.3 79.8 reduce-scatter.1
